TPU v7x, 32 devices: a whole 2x2x4 slice. The times are simulated.
32 devices in a mesh: ctx: 8 (over z, x), tp: 4 (over y, core).
Axes of the slice: x: 2, y: 2, z: 4, core: 2. Of those that a mesh axis runs over, the one named last changes fastest.
Arguments:
- inner_input: bfloat16 [4096, 8192], P('ctx', 'tp'), may hold values from -6 to 6
- state_input: bfloat16 [4096, 2, 1024], P('ctx', None, 'tp'), may hold values from -6 to 6
- gate_input: bfloat16 [4096, 8192], P('ctx', 'tp'), may hold values from -40 to 40
- step_logits: float32 [4096, 128], P('ctx', 'tp'), may hold values from -20 to 1
- conv_inner: bfloat16 [4, 8192], P(None, 'tp'), may hold values from -3 to 3
- conv_states: bfloat16 [4, 2, 1024], P(None, None, 'tp'), may hold values from -3 to 3
- bias_inner: bfloat16 [8192], P('tp'), may hold values from -0.5 to 0.5
- bias_states: bfloat16 [2, 1024], P(None, 'tp'), may hold values from -0.5 to 0.5
- decay_log: float32 [128], P('tp'), may hold values from -0.7 to 0.7
- skip_gain: float32 [128], P('tp'), may hold values from 0.5 to 1.5
- norm_gain: bfloat16 [8192], P('tp'), may hold values from 0.5 to 1.5
- out_weight: bfloat16 [8192, 4096], P('tp'), may hold values from -0.0625 to 0.0625
Outputs:
- layer_out: bfloat16 [4096, 4096], P(('ctx', 'tp'))
All inputs are finite; a program needn't handle non-finite values.
Results may differ from a plain program's by a relative error of at most 0.009.
Values may be sent and summed in bfloat16 or wider, within the bound.
No kernel may reach another device: no remote copies, remote signals or barrier semaphores. Data moves between devices by JAX's collectives and lax.ppermute only.
A program may use at most 128 MiB of HBM per device.

v0:
```python
import jax
import jax.numpy as jnp
from jax import lax
from jax.sharding import PartitionSpec as P

SSM_HEAD_COUNT = 128
HEAD_DIM = 64
STATE = 128
GROUPS = 8
CONV = 4
BLK = 512
epsilon = 1e-05


def shifted(value, axis, by):
    count = lax.axis_size(axis)
    pairs = [(i, i + by) for i in range(count) if 0 <= i + by < count]
    return lax.ppermute(value, axis, pairs)


def conv_silu(padded, weight, offsets, row_count):
    summed = offsets.astype(jnp.float32)
    for k in range(CONV):
        summed = summed + weight[k].astype(jnp.float32) * padded[k : k + row_count].astype(
            jnp.float32
        )
    return lax.optimization_barrier(jax.nn.silu(summed).astype(jnp.bfloat16))


def block_local(carried_in, inputs_block):
    local_state, entry_decay = carried_in
    inner_block, b_block, c_block, step_sizes, log_rates = inputs_block
    length = inner_block.shape[0]
    cumulative = jnp.cumsum(log_rates, axis=0)
    along = jnp.transpose(cumulative, (1, 2, 0))
    causal = lax.broadcasted_iota(jnp.int32, (length, length), 0) >= lax.broadcasted_iota(
        jnp.int32, (length, length), 1
    )
    decays = jnp.exp(jnp.where(causal, along[:, :, :, None] - along[:, :, None, :], -jnp.inf))
    scores = jnp.einsum("ign,jgn->gij", c_block, b_block, preferred_element_type=jnp.float32)
    mixing = (
        decays * scores[:, None] * jnp.transpose(step_sizes, (1, 2, 0))[:, :, None, :]
    ).astype(jnp.bfloat16)
    diagonal = jnp.einsum(
        "ghij,jghp->ighp", mixing, inner_block, preferred_element_type=jnp.float32
    )
    within = jnp.exp(cumulative)
    carried = within[..., None] * jnp.einsum(
        "ign,ghpn->ighp", c_block.astype(jnp.float32), local_state, precision=lax.Precision.HIGHEST
    )
    tail_weight = jnp.exp(cumulative[-1][None] - cumulative) * step_sizes
    weighted = (inner_block * tail_weight[..., None]).astype(jnp.bfloat16)
    block_state = jnp.einsum(
        "jghp,jgn->ghpn", weighted, b_block, preferred_element_type=jnp.float32
    )
    block_decay = jnp.exp(cumulative[-1])
    new_state = block_decay[..., None, None] * local_state + block_state
    return (
        (new_state, entry_decay * block_decay),
        (diagonal + carried, within * entry_decay[None]),
    )


def body(
    inner_input,
    state_input,
    gate_input,
    step_logits,
    conv_inner,
    conv_states,
    bias_inner,
    bias_states,
    decay_log,
    skip_gain,
    norm_gain,
    out_weight,
):
    tokens = inner_input.shape[0]
    margin = CONV - 1
    previous = shifted((inner_input[tokens - margin :], state_input[tokens - margin :]), "ctx", 1)
    inner_conv = conv_silu(
        jnp.concatenate([previous[0], inner_input], axis=0), conv_inner, bias_inner, tokens
    )
    state_conv = conv_silu(
        jnp.concatenate([previous[1], state_input], axis=0), conv_states, bias_states, tokens
    )
    groups_here = state_input.shape[2] // STATE
    per_group = SSM_HEAD_COUNT // GROUPS
    blocks = tokens // BLK
    step_sizes = jax.nn.softplus(step_logits)
    log_rates = -step_sizes * jnp.exp(decay_log)[None]
    c_all = state_conv[:, 1].reshape(blocks, BLK, groups_here, STATE)
    inputs_all = (
        inner_conv.reshape(blocks, BLK, groups_here, per_group, HEAD_DIM),
        state_conv[:, 0].reshape(blocks, BLK, groups_here, STATE),
        c_all,
        step_sizes.reshape(blocks, BLK, groups_here, per_group),
        log_rates.reshape(blocks, BLK, groups_here, per_group),
    )
    start_state = jnp.zeros((groups_here, per_group, HEAD_DIM, STATE), jnp.float32)
    start_decay = jnp.ones((groups_here, per_group), jnp.float32)
    (local_state, device_decay), (partial_heads, factors) = lax.scan(
        block_local, (start_state, start_decay), inputs_all
    )
    own_total = jnp.sum(log_rates, axis=0).reshape(1, groups_here, per_group)
    totals = lax.all_gather(own_total, "ctx", axis=0, tiled=True)
    through = jnp.cumsum(totals, axis=0)
    position = lax.axis_index("ctx")
    before = lax.dynamic_index_in_dim(through - totals, position, 0, keepdims=False)
    shards = lax.all_gather(local_state[None], "ctx", axis=0, tiled=True)
    amount = shards.shape[0]
    anchor = lax.broadcasted_iota(jnp.int32, (amount, 1, 1), 0)
    earlier = anchor < position
    weights_far = jnp.where(earlier, jnp.exp(jnp.where(earlier, before[None] - through, 0.0)), 0.0)
    state_in = jnp.einsum("kgh,kghpn->ghpn", weights_far, shards, precision=lax.Precision.HIGHEST)
    correction = factors[..., None] * jnp.einsum(
        "bign,ghpn->bighp", c_all.astype(jnp.float32), state_in, precision=lax.Precision.HIGHEST
    )
    width_here = groups_here * per_group * HEAD_DIM
    mixed_heads = (partial_heads + correction).reshape(tokens, width_here) + jnp.repeat(
        skip_gain, HEAD_DIM
    )[None] * inner_conv.astype(jnp.float32)
    gated_out = mixed_heads * jax.nn.silu(gate_input.astype(jnp.float32))
    grouped = gated_out.reshape(tokens, groups_here, width_here // groups_here)
    normed = grouped * lax.rsqrt(jnp.mean(grouped * grouped, axis=-1, keepdims=True) + epsilon)
    normed = (normed.reshape(tokens, width_here) * norm_gain.astype(jnp.float32)).astype(
        jnp.bfloat16
    )
    return lax.psum_scatter(
        jnp.dot(normed, out_weight, preferred_element_type=jnp.float32).astype(jnp.bfloat16),
        "tp",
        scatter_dimension=0,
        tiled=True,
    )


def solution(mesh):
    placed = (
        P("ctx", "tp"),
        P("ctx", None, "tp"),
        P("ctx", "tp"),
        P("ctx", "tp"),
        P(None, "tp"),
        P(None, None, "tp"),
        P("tp"),
        P(None, "tp"),
        P("tp"),
        P("tp"),
        P("tp"),
        P("tp", None),
    )
    return jax.shard_map(
        body, mesh=mesh, in_specs=placed, out_specs=P(("ctx", "tp"), None), check_vma=False
    )
```

profile of v0, /device:TPU:0, one launch (start us, length us, event | category | flops | bytes accessed | tf_op | source)
XLA Modules:
  0.0 249.1 jit_solution(14708655856131833193)
XLA Ops:
  6.5 0.8 slice.66
  7.4 0.3 copy.54
  7.7 4.9 %collective-permute-start = (bf16[3,2048]{0,1:T(8,128)(2,1)S(1)}, bf16[3,2048]{0,1:T(8,128)(2,1)S(1)}, u32[]{:S(2)}, u32[]{:S(2)}) collective-permute-start(bf16[3,2048]{0,1:T(8,128)(2,1)S(1)} %copy.54), channel_id=1, source_target_pairs={{0,4},{4,8},{8,12},{12,16},{16,20},{20,24},{24,28},{1,5},{5,9},{9,... | collective-permute-start | bytes 36872 | tf_op jit(solution)/shard_map/ppermute | solution.py:18
  12.6 0.7 slice.76
  13.3 0.2 copy.61
  13.5 3.4 %collective-permute-start.1 = (bf16[3,2,256]{0,2,1:T(8,128)(2,1)S(1)}, bf16[3,2,256]{0,2,1:T(8,128)(2,1)S(1)}, u32[]{:S(2)}, u32[]{:S(2)}) collective-permute-start(bf16[3,2,256]{0,2,1:T(8,128)(2,1)S(1)} %copy.61), channel_id=1, source_target_pairs={{0,4},{4,8},{8,12},{12,16},{16,20},{20,24},{24,28},{1,5},{5,9},{9,... | collective-permute-start | bytes 9224 | tf_op jit(solution)/shard_map/ppermute | solution.py:18
  16.9 0.7 exp.43
  17.6 1.0 fusion.26
  18.6 2.3 reduce-window.6
  20.9 0.1 slice.90
  21.0 0.1 copy.58
  21.1 0.1 bitcast_bitcast_fusion
  21.2 0.2 slice_reduce_fusion
  21.4 0.9 slice_convert_fusion.3
  22.3 0.7 bitcast_convert_fusion.3
  23.0 0.1 fusion.24
  23.1 3.9 %copy.55 = bf16[512,2048]{0,1:T(8,128)(2,1)} copy(bf16[512,2048]{1,0:T(8,128)(2,1)} %param.12) | data formatting | bytes 4194304 | tf_op args[0]
  27.1 0.7 copy.62
  27.9 1.3 multiply_convert_fusion.7
  29.3 9.5 %multiply_convert_fusion.3 = bf16[512,2048]{0,1:T(8,128)(2,1)S(1)} fusion(bf16[512,2048]{0,1:T(8,128)(2,1)} %copy.55, bf16[3,2048]{0,1:T(8,128)(2,1)S(1)} %collective-permute-done, f32[2048]{0:T(1024)S(1)} %bitcast.120, f32[2048]{0:T(1024)S(1)} %bitcast.121, f32[2048]{0:T(1024)S(1)} %bitcast.119, f32[2048]{0:T(1024)S(1)} %bitcast.118, ...), kind=kLoop, calls=%fused_computation.22 | loop fusion | flops 27262976 | bytes 4247552 | tf_op jit(solution)/shard_map/convert_element_type | solution.py:27
  38.8 0.0 copy-start.7
  38.8 0.0 copy-start.5
  38.8 1.7 fusion.16
  40.5 0.0 all-gather.3.cloned.1.call-update
  40.6 0.0 reduce-scatter.2.cloned.1.call-start
  40.6 0.1 reshape.66
  40.7 20.8 %all_gather.6 = f32[8,2,16]{2,1,0:T(2,128)S(1)} all-gather(f32[1,2,16]{2,1,0:T(2,128)S(1)} %reshape.66), channel_id=1, replica_groups=mesh['ctx'=8,'tp'=4] {'ctx'}, dimensions={0}, use_global_device_ids=true | all-gather | bytes 1152 | tf_op jit(solution)/shard_map/all_gather | solution.py:106
  61.5 0.1 select_bitcast_fusion
  61.6 0.1 copy.74
  61.7 3.9 %copy.69 = bf16[512,2048]{0,1:T(8,128)(2,1)} copy(bf16[512,2048]{1,0:T(8,128)(2,1)} %param.14) | data formatting | bytes 4194304 | tf_op args[2]
  65.6 0.1 broadcast_in_dim.87
  65.7 0.1 mul.293
  65.8 0.1 iota_compare_fusion
  65.8 0.5 fusion.29
  66.3 3.7 %fusion.19 = f32[2,16,64,512]{3,2,1,0:T(8,128)} fusion(bf16[512,2,128,1]{0,2,3,1:T(8,128)(2,1)S(1)} %bitcast.109), kind=kOutput, calls=%fused_computation.42 | convolution fusion | flops 1610612736 | bytes 4456448 | tf_op jit(solution)/shard_map/while/body/eval_jaxpr/ign,ghpn->ighp/dot_general | solution.py:48
  70.1 10.4 %fusion = f32[2,16,64,512]{3,2,1,0:T(8,128)} fusion(bf16[512,2,16,64]{0,3,2,1:T(8,128)(2,1)S(1)} %bitcast.106, f32[2,16,512]{2,1,0:T(8,128)S(1)} %bitcast.116, f32[2,512,512]{2,1,0:T(8,128)S(1)} %fusion.29, f32[2,16,512]{2,1,0:T(8,128)S(1)} %get-tuple-element.44, pred[512,512]{1,0:T(8,128)(4,1)S(1)} %iota_compare_fusion), kind=kOutput, calls=%fused_computation.1 | convolution fusion | flops 1115684864 | bytes 8781824 | tf_op jit(solution)/shard_map/while/body/eval_jaxpr/ghij,jghp->ighp/dot_general | solution.py:44
  80.5 86.0 %all-gather.3.cloned.1.call-done = f32[16,16,64,128]{3,2,1,0:T(8,128)} async-done(((f32[2,16,64,128]{3,2,1,0:T(8,128)}), f32[16,16,64,128]{3,2,1,0:T(8,128)}) %all-gather.3.cloned.1.call-update) | async-done | bytes 8388624 | tf_op jit(solution)/shard_map/all_gather | solution.py:110
  166.5 15.7 %fusion.2 = f32[2,16,1,64,128]{4,2,3,1,0:T(1,128)S(1)} fusion(f32[8,2,16,1,1]{0,3,4,2,1:T(1,128)S(1)} %copy.74, f32[8,2,16,64,128]{4,3,2,1,0:T(8,128)} %bitcast.107), kind=kOutput, calls=%fused_computation.3 | convolution fusion | flops 25165824 | bytes 9438208 | tf_op jit(solution)/shard_map/kgh,kghpn->ghpn/dot_general | solution.py:115
  182.2 0.0 slice-start
  182.3 2.1 fusion.8
  184.4 0.0 slice-start.2
  184.4 2.1 bitcast_reduce_fusion
  186.5 0.4 fusion.10
  187.0 0.7 slice-done.2
  187.7 1.2 slice-done.3
  188.9 10.6 %convolution_convert_fusion = bf16[512,4096]{1,0:T(8,128)(2,1)} fusion(bf16[512,2048]{0,1:T(8,128)(2,1)S(1)} %fusion.10, bf16[2048,4096]{1,0:T(8,128)(2,1)S(1)} %bitcast.124), kind=kOutput, calls=%fused_computation.5 | convolution fusion | flops 8592031744 | bytes 23068672 | tf_op jit(solution)/shard_map/dot_general | solution.py:130
  199.4 0.0 reduce-scatter.2.cloned.1.call-update
  199.5 42.8 %reduce-scatter.2.cloned.1.call-done = bf16[128,4096]{1,0:T(8,128)(2,1)} async-done(((bf16[512,4096]{1,0:T(8,128)(2,1)}), bf16[128,4096]{1,0:T(8,128)(2,1)}) %reduce-scatter.2.cloned.1.call-update) | async-done | bytes 1048592 | tf_op jit(solution)/shard_map/reduce_scatter | solution.py:129
  (35 shorter events, 0.2 us)
Async XLA Ops:
  6.5 20.5 %copy-start.3 = (bf16[512,2,256]{2,1,0:T(2,128)(2,1)S(1)}, bf16[512,2,256]{2,1,0:T(2,128)(2,1)}, u32[]{:S(2)}) copy-start(bf16[512,2,256]{2,1,0:T(2,128)(2,1)} %param.13) | copy-start | bytes 1572868
  6.5 21.3 %copy-start.4 = (bf16[2048]{0:T(1024)(128)(2,1)S(1)}, bf16[2048]{0:T(1024)(128)(2,1)}, u32[]{:S(2)}) copy-start(bf16[2048]{0:T(1024)(128)(2,1)} %param.18) | copy-start | bytes 12292
  6.5 21.3 %copy-start.6 = (bf16[2,256]{1,0:T(2,128)(2,1)S(1)}, bf16[2,256]{1,0:T(2,128)(2,1)}, u32[]{:S(2)}) copy-start(bf16[2,256]{1,0:T(2,128)(2,1)} %param.19) | copy-start | bytes 3076
  6.5 160.0 %all-gather.3.cloned.1.call-start = ((), (), s32[]{:S(2)}) async-start(), calls=%async_computation.2 | async-start | bytes 9437184 | tf_op jit(solution)/shard_map/all_gather | solution.py:110
  7.7 21.6 %collective-permute-start = (bf16[3,2048]{0,1:T(8,128)(2,1)S(1)}, bf16[3,2048]{0,1:T(8,128)(2,1)S(1)}, u32[]{:S(2)}, u32[]{:S(2)}) collective-permute-start(bf16[3,2048]{0,1:T(8,128)(2,1)S(1)} %copy.54), channel_id=1, source_target_pairs={{0,4},{4,8},{8,12},{12,16},{16,20},{20,24},{24,28},{1,5},{5,9},{9,... | collective-permute-start | bytes 36872 | tf_op jit(solution)/shard_map/ppermute | solution.py:18
  13.5 14.4 %collective-permute-start.1 = (bf16[3,2,256]{0,2,1:T(8,128)(2,1)S(1)}, bf16[3,2,256]{0,2,1:T(8,128)(2,1)S(1)}, u32[]{:S(2)}, u32[]{:S(2)}) collective-permute-start(bf16[3,2,256]{0,2,1:T(8,128)(2,1)S(1)} %copy.61), channel_id=1, source_target_pairs={{0,4},{4,8},{8,12},{12,16},{16,20},{20,24},{24,28},{1,5},{5,9},{9,... | collective-permute-start | bytes 9224 | tf_op jit(solution)/shard_map/ppermute | solution.py:18
  38.8 26.8 %copy-start.7 = (f32[32]{0:T(128)S(1)}, f32[32]{0:T(128)}, u32[]{:S(2)}) copy-start(f32[32]{0:T(128)} %param.21) | copy-start | bytes 388
  38.8 26.9 %copy-start.5 = (bf16[2048]{0:T(1024)(128)(2,1)S(1)}, bf16[2048]{0:T(1024)(128)(2,1)}, u32[]{:S(2)}) copy-start(bf16[2048]{0:T(1024)(128)(2,1)} %param.22) | copy-start | bytes 12292
  40.6 201.7 %reduce-scatter.2.cloned.1.call-start = ((), (), s32[]{:S(2)}) async-start(), calls=%async_computation.1 | async-start | bytes 5242880 | tf_op jit(solution)/shard_map/reduce_scatter | solution.py:129
  166.5 15.7 %copy-start = (f32[2,16,64,512]{3,2,1,0:T(8,128)S(1)}, f32[2,16,64,512]{3,2,1,0:T(8,128)}, u32[]{:S(2)}) copy-start(f32[2,16,64,512]{3,2,1,0:T(8,128)} %fusion.19) | copy-start | bytes 12582916
  166.5 15.7 %copy-start.2 = (f32[2,16,64,512]{3,2,1,0:T(8,128)S(1)}, f32[2,16,64,512]{3,2,1,0:T(8,128)}, u32[]{:S(2)}) copy-start(f32[2,16,64,512]{3,2,1,0:T(8,128)} %fusion) | copy-start | bytes 12582916
  182.2 2.2 copy-start.1
  182.2 4.7 %slice-start = ((s8[16777216]{0:T(1024)(128)(4,1)}), s8[4194304]{0:T(1024)(128)(4,1)S(1)}, s32[]{:S(2)}) async-start(s8[16777216]{0:T(1024)(128)(4,1)} %bitcast.123), calls=%async_computation.3 | async-start | bytes 8388608
  182.2 4.7 %slice-start.1 = ((s8[16777216]{0:T(1024)(128)(4,1)}), s8[4194304]{0:T(1024)(128)(4,1)S(1)}, s32[]{:S(2)}) async-start(s8[16777216]{0:T(1024)(128)(4,1)} %bitcast.123), calls=%async_computation.4 | async-start | bytes 8388608
  184.4 3.3 %slice-start.2 = ((s8[16777216]{0:T(1024)(128)(4,1)}), s8[4194304]{0:T(1024)(128)(4,1)S(1)}, s32[]{:S(2)}) async-start(s8[16777216]{0:T(1024)(128)(4,1)} %bitcast.123), calls=%async_computation.5 | async-start | bytes 8388608
  184.4 4.4 %slice-start.3 = ((s8[16777216]{0:T(1024)(128)(4,1)}), s8[4194304]{0:T(1024)(128)(4,1)S(1)}, s32[]{:S(2)}) async-start(s8[16777216]{0:T(1024)(128)(4,1)} %bitcast.123), calls=%async_computation.6 | async-start | bytes 8388608
Sparse Core Ops, SparseCore 0:
  40.7 125.7 all-gather.2
  199.6 42.6 reduce-scatter.1
where the time goes:
time: 250 us; the launch traced here: 249 us
  waiting for transfers between devices  129 us (52%)
  matrix products  44.7 us (18%)
  blocking collectives  20.8 us (8%)
  other arithmetic  18.7 us (7%)
  local copies, waits for them, and re-layouts  13.9 us (6%)
  between operations  13.7 us (5%)
  starting transfers between devices  8.35 us (3%)
    all_gather x1, waiting for transfers between devices, body(): shards = lax.all_gather(local_state[None], 'ctx', axis=0, tiled=True)  86 us
    reduce_scatter x1, waiting for transfers between devices, body(): lax.psum_scatter(jnp.dot(normed, out_weight, preferred_element_type=jnp.f...  42.8 us
    all_gather x1, blocking collectives, body(): totals = lax.all_gather(own_total, 'ctx', axis=0, tiled=True)  20.8 us
    dot_general x1, matrix products, body(): jnp.einsum('kgh,kghpn->ghpn', weights_far, shards, precision=lax.Precisio...  15.7 us
    convert_element_type x2, other arithmetic, conv_silu(): return lax.optimization_barrier(jax.nn.silu(summed).astype(jnp.bfloat16))  10.9 us
    dot_general x1, matrix products, body(): jnp.dot(normed, out_weight, preferred_element_type=jnp.float32)  10.6 us
    unnamed x27, local copies, waits for them, and re-layouts  10.5 us
    dot_general x1, matrix products, block_local(): jnp.einsum('ghij,jghp->ighp', mixing, inner_block, preferred_element_type...  10.4 us
  transfers between devices with their start and end apart: 4, of which 2 were waited for; matrix products, arithmetic and copies ran while one was open for 13% of the time, Pallas kernels for 0%

commit v1 on v0

--- a/solution.py
+++ b/solution.py
@@ -107,7 +107,18 @@
     through = jnp.cumsum(totals, axis=0)
     position = lax.axis_index("ctx")
     before = lax.dynamic_index_in_dim(through - totals, position, 0, keepdims=False)
-    shards = lax.all_gather(local_state[None], "ctx", axis=0, tiled=True)
+    ways = lax.axis_size("ctx")
+    up = [(d, (d + 1) % ways) for d in range(ways)]
+    down = [(d, (d - 1) % ways) for d in range(ways)]
+    earlier_2, later = ([local_state[None]], [local_state[None]])
+    for _ in range(ways // 2):
+        earlier_2.append(lax.ppermute(earlier_2[-1], "ctx", up))
+    for _ in range((ways - 1) // 2):
+        later.append(lax.ppermute(later[-1], "ctx", down))
+    line = jnp.concatenate([*earlier_2[::-1], *later[1:]], axis=0)
+    shards = jnp.roll(
+        line, (lax.axis_index("ctx") - ways // 2) * local_state[None].shape[0], axis=0
+    )
     amount = shards.shape[0]
     anchor = lax.broadcasted_iota(jnp.int32, (amount, 1, 1), 0)
     earlier = anchor < position

time: 250 us -> 328 us (1.31)
  local copies, waits for them, and re-layouts: 13.9 us -> 50.9 us
  starting transfers between devices: 8.35 us -> 29.6 us
  blocking collectives: 20.8 us -> 33.8 us
  waiting for transfers between devices: 129 us -> 138 us
  matrix products: 44.7 us -> 38.3 us
  other arithmetic: 18.7 us -> 22 us
    ppermute x0 -> x7, waiting for transfers between devices: none -> 92 us  [the longest x4 72 us: body(): earlier_2.append(lax.ppermute(earlier_2[-1], 'ctx', up))]
    all_gather x1 -> x0, waiting for transfers between devices: 86 us -> none  [body(): shards = lax.all_gather(local_state[None], 'ctx', axis=0, tiled=True)]
    unnamed x27 -> x44, local copies, waits for them, and re-layouts: 10.5 us -> 39 us
    ppermute x0 -> x7, starting transfers between devices: none -> 21.3 us  [the longest x4 16.6 us: body(): earlier_2.append(lax.ppermute(earlier_2[-1], 'ctx', up))]
    all_gather x1, blocking collectives: 20.8 us -> 33.8 us  [body(): totals = lax.all_gather(own_total, 'ctx', axis=0, tiled=True)]
    dot_general x1, matrix products: 15.7 us -> 11.1 us  [body(): jnp.einsum('kgh,kghpn->ghpn', weights_far, shards, precision=lax.Precisio...]
    dynamic_slice x0 -> x1, local copies, waits for them, and re-layouts: none -> 4.23 us  [body(): jnp.roll(line, (lax.axis_index('ctx') - ways // 2) * local_state[None].sh...]
  transfers between devices with their start and end apart: 4 -> 10, of which waited for: 2 -> 5; matrix products, arithmetic and copies ran while one was open for 13% -> 16% of each run, Pallas kernels for 0% -> 0%
where the time goes in v1:
time: 328 us; the launch traced here: 326 us
  waiting for transfers between devices  138 us (42%)
  local copies, waits for them, and re-layouts  50.9 us (16%)
  matrix products  38.3 us (12%)
  blocking collectives  33.8 us (10%)
  starting transfers between devices  29.6 us (9%)
  other arithmetic  22 us (7%)
  between operations  13.7 us (4%)
    ppermute x4, waiting for transfers between devices, body(): earlier_2.append(lax.ppermute(earlier_2[-1], 'ctx', up))  72 us
    reduce_scatter x1, waiting for transfers between devices, body(): lax.psum_scatter(jnp.dot(normed, out_weight, preferred_element_type=jnp.f...  46.1 us
    unnamed x44, local copies, waits for them, and re-layouts  39 us
    all_gather x1, blocking collectives, body(): totals = lax.all_gather(own_total, 'ctx', axis=0, tiled=True)  33.8 us
    ppermute x3, waiting for transfers between devices, body(): later.append(lax.ppermute(later[-1], 'ctx', down))  20 us
    ppermute x4, starting transfers between devices, body(): earlier_2.append(lax.ppermute(earlier_2[-1], 'ctx', up))  16.6 us
    dot_general x1, matrix products, body(): jnp.einsum('kgh,kghpn->ghpn', weights_far, shards, precision=lax.Precisio...  11.1 us
    convert_element_type x2, other arithmetic, conv_silu(): return lax.optimization_barrier(jax.nn.silu(summed).astype(jnp.bfloat16))  11 us
  transfers between devices with their start and end apart: 10, of which 5 were waited for; matrix products, arithmetic and copies ran while one was open for 16% of the time, Pallas kernels for 0%

profile of v1, /device:TPU:0, one launch (start us, length us, event | category | flops | bytes accessed | tf_op | source)
XLA Modules:
  0.0 326.4 jit_solution(14983972047085837323)
XLA Ops:
  7.7 4.9 %collective-permute-start = (bf16[3,2048]{0,1:T(8,128)(2,1)S(1)}, bf16[3,2048]{0,1:T(8,128)(2,1)S(1)}, u32[]{:S(2)}, u32[]{:S(2)}) collective-permute-start(bf16[3,2048]{0,1:T(8,128)(2,1)S(1)} %copy.54), channel_id=1, source_target_pairs={{0,4},{4,8},{8,12},{12,16},{16,20},{20,24},{24,28},{1,5},{5,9},{9,... | collective-permute-start | bytes 36872 | tf_op jit(solution)/shard_map/ppermute | solution.py:18
  13.5 3.4 %collective-permute-start.1 = (bf16[3,2,256]{0,2,1:T(8,128)(2,1)S(1)}, bf16[3,2,256]{0,2,1:T(8,128)(2,1)S(1)}, u32[]{:S(2)}, u32[]{:S(2)}) collective-permute-start(bf16[3,2,256]{0,2,1:T(8,128)(2,1)S(1)} %copy.61), channel_id=1, source_target_pairs={{0,4},{4,8},{8,12},{12,16},{16,20},{20,24},{24,28},{1,5},{5,9},{9,... | collective-permute-start | bytes 9224 | tf_op jit(solution)/shard_map/ppermute | solution.py:18
  17.6 1.0 fusion.27
  18.6 2.3 reduce-window.6
  24.4 3.9 %copy.55 = bf16[512,2048]{0,1:T(8,128)(2,1)} copy(bf16[512,2048]{1,0:T(8,128)(2,1)} %param.12) | data formatting | bytes 4194304 | tf_op args[0]
  29.1 1.3 multiply_convert_fusion.9
  30.5 9.7 %multiply_convert_fusion.3 = bf16[512,2048]{0,1:T(8,128)(2,1)S(1)} fusion(bf16[512,2048]{0,1:T(8,128)(2,1)} %copy.55, bf16[3,2048]{0,1:T(8,128)(2,1)S(1)} %collective-permute-done, f32[2048]{0:T(1024)S(1)} %bitcast.120, f32[2048]{0:T(1024)S(1)} %bitcast.121, f32[2048]{0:T(1024)S(1)} %bitcast.119, f32[2048]{0:T(1024)S(1)} %bitcast.118, ...), kind=kLoop, calls=%fused_computation.22 | loop fusion | flops 27262976 | bytes 4247552 | tf_op jit(solution)/shard_map/convert_element_type | solution.py:27
  40.9 1.5 collective-permute-start.2
  42.5 3.2 collective-permute-start.6
  45.7 41.1 %collective-permute-done.2 = f32[1,2,16,64,128]{4,3,2,1,0:T(8,128)} collective-permute-done((f32[1,2,16,64,128]{4,3,2,1,0:T(8,128)S(1)}, f32[1,2,16,64,128]{4,3,2,1,0:T(8,128)}, u32[]{:S(2)}, u32[]{:S(2)}) %collective-permute-start.2) | collective-permute-done | bytes 1048608 | tf_op jit(solution)/shard_map/ppermute | solution.py:115
  86.8 2.6 collective-permute-start.3
  89.5 33.8 %all_gather.3 = f32[8,2,16]{2,1,0:T(2,128)S(1)} all-gather(f32[1,2,16]{2,1,0:T(2,128)S(1)} %reshape.66), channel_id=1, replica_groups=mesh['ctx'=8,'tp'=4] {'ctx'}, dimensions={0}, use_global_device_ids=true | all-gather | bytes 1152 | tf_op jit(solution)/shard_map/all_gather | solution.py:106
  123.3 1.4 collective-permute-start.7
  124.8 10.0 %collective-permute-start.4 = (f32[1,2,16,64,128]{4,3,2,1,0:T(8,128)}, f32[1,2,16,64,128]{4,3,2,1,0:T(8,128)}, u32[]{:S(2)}, u32[]{:S(2)}) collective-permute-start(f32[1,2,16,64,128]{4,3,2,1,0:T(8,128)} %collective-permute-done.3), channel_id=1, source_target_pairs={{0,4},{4,8},{8,12},{12,16},{16,20},{20,24},{24,28},{28,0},{1,5},{5... | collective-permute-start | bytes 3145736 | tf_op jit(solution)/shard_map/ppermute | solution.py:115
  136.2 3.9 %copy.69 = bf16[512,2048]{0,1:T(8,128)(2,1)} copy(bf16[512,2048]{1,0:T(8,128)(2,1)} %param.14) | data formatting | bytes 4194304 | tf_op args[2]
  140.1 1.3 broadcast_in_dim.88
  141.4 1.4 mul.293
  142.8 1.3 convert_element_type.99
  144.2 1.4 fusion.30
  145.6 1.8 fusion.20
  147.4 20.0 %collective-permute-done.7 = f32[1,2,16,64,128]{4,3,2,1,0:T(8,128)} collective-permute-done((f32[1,2,16,64,128]{4,3,2,1,0:T(8,128)}, f32[1,2,16,64,128]{4,3,2,1,0:T(8,128)}, u32[]{:S(2)}, u32[]{:S(2)}) %collective-permute-start.7) | collective-permute-done | bytes 1048608 | tf_op jit(solution)/shard_map/ppermute | solution.py:117
  167.4 22.9 %collective-permute-done.4 = f32[1,2,16,64,128]{4,3,2,1,0:T(8,128)} collective-permute-done((f32[1,2,16,64,128]{4,3,2,1,0:T(8,128)}, f32[1,2,16,64,128]{4,3,2,1,0:T(8,128)}, u32[]{:S(2)}, u32[]{:S(2)}) %collective-permute-start.4) | collective-permute-done | bytes 1048608 | tf_op jit(solution)/shard_map/ppermute | solution.py:115
  190.3 2.5 collective-permute-start.5
  192.8 9.9 %fusion = f32[2,16,64,512]{3,2,1,0:T(8,128)S(1)} fusion(bf16[512,2,16,64]{0,3,2,1:T(8,128)(2,1)S(1)} %bitcast.107, f32[2,16,512]{2,1,0:T(8,128)S(1)} %bitcast.116, f32[2,512,512]{2,1,0:T(8,128)S(1)} %fusion.30, f32[2,16,512]{2,1,0:T(8,128)S(1)} %copy-done.3, pred[512,512]{1,0:T(8,128)(4,1)S(1)} %iota_compare_fusion), kind=kOutput, calls=%fused_computation.1 | convolution fusion | flops 1115684864 | bytes 8781824 | tf_op jit(solution)/shard_map/while/body/eval_jaxpr/ghij,jghp->ighp/dot_general | solution.py:44
  202.7 8.0 %collective-permute-done.5 = f32[1,2,16,64,128]{4,3,2,1,0:T(8,128)S(1)} collective-permute-done((f32[1,2,16,64,128]{4,3,2,1,0:T(8,128)}, f32[1,2,16,64,128]{4,3,2,1,0:T(8,128)S(1)}, u32[]{:S(2)}, u32[]{:S(2)}) %collective-permute-start.5) | collective-permute-done | bytes 1048608 | tf_op jit(solution)/shard_map/ppermute | solution.py:115
  210.7 1.1 constant_dynamic-update-slice_fusion.15
  211.7 2.3 constant_dynamic-update-slice_fusion.14
  214.0 2.3 constant_dynamic-update-slice_fusion.13
  216.3 2.3 constant_dynamic-update-slice_fusion.12
  218.7 1.0 constant_dynamic-update-slice_fusion.11
  219.7 2.3 constant_dynamic-update-slice_fusion.10
  222.1 2.3 constant_dynamic-update-slice_fusion.9
  224.4 1.1 constant_dynamic-update-slice_fusion.8
  225.5 1.1 constant_dynamic-update-slice_fusion.7
  226.6 2.3 constant_dynamic-update-slice_fusion.6
  228.9 2.3 constant_dynamic-update-slice_fusion.5
  231.3 2.3 constant_dynamic-update-slice_fusion.4
  233.6 1.1 constant_dynamic-update-slice_fusion.3
  234.7 2.3 constant_dynamic-update-slice_fusion.2
  237.0 2.3 constant_dynamic-update-slice_fusion.1
  239.3 1.1 constant_dynamic-update-slice_fusion
  240.4 4.2 %constant_dynamic-slice_fusion = f32[8,2,16,64,128]{4,3,2,1,0:T(8,128)S(1)} fusion(f32[16,2,16,64,128]{4,3,2,1,0:T(8,128)} %constant_dynamic-update-slice_fusion, s32[]{:T(128)S(6)} %select_n.39), kind=kLoop, calls=%fused_computation.82 | loop fusion | bytes 16777220 | tf_op jit(solution)/shard_map/jit(_roll_dynamic)/dynamic_slice | solution.py:119
  244.6 11.1 %fusion.2 = f32[2,16,1,64,128]{4,2,3,1,0:T(1,128)S(1)} fusion(f32[8,2,16,1,1]{0,3,4,2,1:T(1,128)S(1)} %copy.74, f32[8,2,16,64,128]{4,3,2,1,0:T(8,128)S(1)} %constant_dynamic-slice_fusion), kind=kOutput, calls=%fused_computation.3 | convolution fusion | flops 25165824 | bytes 9438208 | tf_op jit(solution)/shard_map/kgh,kghpn->ghpn/dot_general | solution.py:126
  255.8 2.4 fusion.8
  258.3 2.1 bitcast_reduce_fusion
  261.2 1.2 slice-done.3
  262.4 11.0 %convolution_convert_fusion = bf16[512,4096]{1,0:T(8,128)(2,1)} fusion(bf16[512,2048]{0,1:T(8,128)(2,1)S(1)} %fusion.10, bf16[2048,4096]{1,0:T(8,128)(2,1)S(1)} %bitcast.124), kind=kOutput, calls=%fused_computation.5 | convolution fusion | flops 8592031744 | bytes 23068672 | tf_op jit(solution)/shard_map/dot_general | solution.py:141
  273.4 46.1 %reduce-scatter.2.cloned.1.call-done = bf16[128,4096]{1,0:T(8,128)(2,1)} async-done(((bf16[512,4096]{1,0:T(8,128)(2,1)}), bf16[128,4096]{1,0:T(8,128)(2,1)}) %reduce-scatter.2.cloned.1.call-update) | async-done | bytes 1048592 | tf_op jit(solution)/shard_map/reduce_scatter | solution.py:140
  (65 shorter events, 10.2 us)
Async XLA Ops:
  6.5 21.8 %copy-start.2 = (bf16[512,2,256]{2,1,0:T(2,128)(2,1)S(1)}, bf16[512,2,256]{2,1,0:T(2,128)(2,1)}, u32[]{:S(2)}) copy-start(bf16[512,2,256]{2,1,0:T(2,128)(2,1)} %param.13) | copy-start | bytes 1572868
  6.5 22.5 %copy-start.7 = (bf16[2048]{0:T(1024)(128)(2,1)S(1)}, bf16[2048]{0:T(1024)(128)(2,1)}, u32[]{:S(2)}) copy-start(bf16[2048]{0:T(1024)(128)(2,1)} %param.18) | copy-start | bytes 12292
  6.5 22.5 %copy-start.8 = (bf16[2,256]{1,0:T(2,128)(2,1)S(1)}, bf16[2,256]{1,0:T(2,128)(2,1)}, u32[]{:S(2)}) copy-start(bf16[2,256]{1,0:T(2,128)(2,1)} %param.19) | copy-start | bytes 3076
  6.5 313.0 %reduce-scatter.2.cloned.1.call-start = ((), (), s32[]{:S(2)}) async-start(), calls=%async_computation.1 | async-start | bytes 5242880 | tf_op jit(solution)/shard_map/reduce_scatter | solution.py:140
  7.7 22.8 %collective-permute-start = (bf16[3,2048]{0,1:T(8,128)(2,1)S(1)}, bf16[3,2048]{0,1:T(8,128)(2,1)S(1)}, u32[]{:S(2)}, u32[]{:S(2)}) collective-permute-start(bf16[3,2048]{0,1:T(8,128)(2,1)S(1)} %copy.54), channel_id=1, source_target_pairs={{0,4},{4,8},{8,12},{12,16},{16,20},{20,24},{24,28},{1,5},{5,9},{9,... | collective-permute-start | bytes 36872 | tf_op jit(solution)/shard_map/ppermute | solution.py:18
  13.5 15.7 %collective-permute-start.1 = (bf16[3,2,256]{0,2,1:T(8,128)(2,1)S(1)}, bf16[3,2,256]{0,2,1:T(8,128)(2,1)S(1)}, u32[]{:S(2)}, u32[]{:S(2)}) collective-permute-start(bf16[3,2,256]{0,2,1:T(8,128)(2,1)S(1)} %copy.61), channel_id=1, source_target_pairs={{0,4},{4,8},{8,12},{12,16},{16,20},{20,24},{24,28},{1,5},{5,9},{9,... | collective-permute-start | bytes 9224 | tf_op jit(solution)/shard_map/ppermute | solution.py:18
  29.1 11.1 %copy-start.4 = (f32[512,2,16]{0,2,1:T(8,128)S(1)}, f32[512,2,16]{0,2,1:T(8,128)}, u32[]{:S(2)}) copy-start(f32[512,2,16]{0,2,1:T(8,128)} %get-tuple-element.40) | copy-start | bytes 196612
  30.5 56.3 %copy-start.1 = (bf16[512,1,256]{0,2,1:T(8,128)(2,1)}, bf16[512,1,256]{0,2,1:T(8,128)(2,1)S(1)}, u32[]{:S(2)}) copy-start(bf16[512,1,256]{0,2,1:T(8,128)(2,1)S(1)} %get-tuple-element.27) | copy-start | bytes 786436
  40.9 45.9 %collective-permute-start.2 = (f32[1,2,16,64,128]{4,3,2,1,0:T(8,128)S(1)}, f32[1,2,16,64,128]{4,3,2,1,0:T(8,128)}, u32[]{:S(2)}, u32[]{:S(2)}) collective-permute-start(f32[1,2,16,64,128]{4,3,2,1,0:T(8,128)S(1)} %fusion.17), channel_id=1, source_target_pairs={{0,4},{4,8},{8,12},{12,16},{16,20},{20,24},{24,28},{28,0},{1,5},{5... | collective-permute-start | bytes 3145736 | tf_op jit(solution)/shard_map/ppermute | solution.py:115
  42.5 80.8 %collective-permute-start.6 = (f32[1,2,16,64,128]{4,3,2,1,0:T(8,128)S(1)}, f32[1,2,16,64,128]{4,3,2,1,0:T(8,128)}, u32[]{:S(2)}, u32[]{:S(2)}) collective-permute-start(f32[1,2,16,64,128]{4,3,2,1,0:T(8,128)S(1)} %fusion.17), channel_id=1, source_target_pairs={{0,28},{4,0},{8,4},{12,8},{16,12},{20,16},{24,20},{28,24},{1,29},{... | collective-permute-start | bytes 3145736 | tf_op jit(solution)/shard_map/ppermute | solution.py:117
  86.8 37.9 %collective-permute-start.3 = (f32[1,2,16,64,128]{4,3,2,1,0:T(8,128)}, f32[1,2,16,64,128]{4,3,2,1,0:T(8,128)}, u32[]{:S(2)}, u32[]{:S(2)}) collective-permute-start(f32[1,2,16,64,128]{4,3,2,1,0:T(8,128)} %collective-permute-done.2), channel_id=1, source_target_pairs={{0,4},{4,8},{8,12},{12,16},{16,20},{20,24},{24,28},{28,0},{1,5},{5... | collective-permute-start | bytes 3145736 | tf_op jit(solution)/shard_map/ppermute | solution.py:115
  123.3 44.0 %collective-permute-start.7 = (f32[1,2,16,64,128]{4,3,2,1,0:T(8,128)}, f32[1,2,16,64,128]{4,3,2,1,0:T(8,128)}, u32[]{:S(2)}, u32[]{:S(2)}) collective-permute-start(f32[1,2,16,64,128]{4,3,2,1,0:T(8,128)} %collective-permute-done.6), channel_id=1, source_target_pairs={{0,28},{4,0},{8,4},{12,8},{16,12},{20,16},{24,20},{28,24},{1,29},{... | collective-permute-start | bytes 3145736 | tf_op jit(solution)/shard_map/ppermute | solution.py:117
  124.8 65.6 %collective-permute-start.4 = (f32[1,2,16,64,128]{4,3,2,1,0:T(8,128)}, f32[1,2,16,64,128]{4,3,2,1,0:T(8,128)}, u32[]{:S(2)}, u32[]{:S(2)}) collective-permute-start(f32[1,2,16,64,128]{4,3,2,1,0:T(8,128)} %collective-permute-done.3), channel_id=1, source_target_pairs={{0,4},{4,8},{8,12},{12,16},{16,20},{20,24},{24,28},{28,0},{1,5},{5... | collective-permute-start | bytes 3145736 | tf_op jit(solution)/shard_map/ppermute | solution.py:115
  144.1 48.7 %copy-start.3 = (f32[2,16,512]{2,1,0:T(8,128)S(1)}, f32[2,16,512]{2,1,0:T(8,128)}, u32[]{:S(2)}) copy-start(f32[2,16,512]{2,1,0:T(8,128)} %get-tuple-element.44) | copy-start | bytes 196612
  167.4 57.1 %collective-permute-start.8 = (f32[1,2,16,64,128]{4,3,2,1,0:T(8,128)}, f32[1,2,16,64,128]{4,3,2,1,0:T(8,128)S(1)}, u32[]{:S(2)}, u32[]{:S(2)}) collective-permute-start(f32[1,2,16,64,128]{4,3,2,1,0:T(8,128)} %collective-permute-done.7), channel_id=1, source_target_pairs={{0,28},{4,0},{8,4},{12,8},{16,12},{20,16},{24,20},{28,24},{1,29},{... | collective-permute-start | bytes 3145736 | tf_op jit(solution)/shard_map/ppermute | solution.py:117
  190.3 20.4 %collective-permute-start.5 = (f32[1,2,16,64,128]{4,3,2,1,0:T(8,128)}, f32[1,2,16,64,128]{4,3,2,1,0:T(8,128)S(1)}, u32[]{:S(2)}, u32[]{:S(2)}) collective-permute-start(f32[1,2,16,64,128]{4,3,2,1,0:T(8,128)} %collective-permute-done.4), channel_id=1, source_target_pairs={{0,4},{4,8},{8,12},{12,16},{16,20},{20,24},{24,28},{28,0},{1,5},{5... | collective-permute-start | bytes 3145736 | tf_op jit(solution)/shard_map/ppermute | solution.py:115
  255.7 2.5 copy-start
  255.8 2.5 copy-start.5
  255.8 5.0 %slice-start = ((s8[16777216]{0:T(1024)(128)(4,1)}), s8[4194304]{0:T(1024)(128)(4,1)S(1)}, s32[]{:S(2)}) async-start(s8[16777216]{0:T(1024)(128)(4,1)} %bitcast.123), calls=%async_computation.2 | async-start | bytes 8388608
  255.8 5.0 %slice-start.1 = ((s8[16777216]{0:T(1024)(128)(4,1)}), s8[4194304]{0:T(1024)(128)(4,1)S(1)}, s32[]{:S(2)}) async-start(s8[16777216]{0:T(1024)(128)(4,1)} %bitcast.123), calls=%async_computation.3 | async-start | bytes 8388608
  258.2 2.1 copy-start.6
  258.2 3.0 slice-start.2
  258.2 4.2 %slice-start.3 = ((s8[16777216]{0:T(1024)(128)(4,1)}), s8[4194304]{0:T(1024)(128)(4,1)S(1)}, s32[]{:S(2)}) async-start(s8[16777216]{0:T(1024)(128)(4,1)} %bitcast.123), calls=%async_computation.5 | async-start | bytes 8388608
Sparse Core Ops, SparseCore 0:
  273.6 45.8 reduce-scatter.1
